TPU v7x, 32 devices: a whole 2x2x4 slice. The times are simulated.
32 devices in a mesh: band: 2 (over x), spk: 16 (over z, y, core).
Axes of the slice: x: 2, y: 2, z: 4, core: 2. Of those that a mesh axis runs over, the one named last changes fastest.
Arguments:
- direction: float32 [64, 128, 128], P(('band', 'spk')), parts along dimension 0, may hold values from -6 to 6
- plant: bfloat16 [832, 2, 128, 128], P(('band', 'spk')), parts along dimension 0
- tile_pairs: int32 [832, 2], P(('band', 'spk')), parts along dimension 0, may hold values from 0 to 127, as said below
- mic_weight: float32 [2, 128, 128], P('band', 'spk'), parts along dimension 0, may hold values from 0.3 to 3
Outputs:
- hessian_vector: float32 [64, 128, 128], P(('band', 'spk')), parts along dimension 0
There are 2 independent parts, one for each index of `band`. A program takes and returns all parts, laid end to end along the dimension named above; each array names one. Nothing has to cross between parts.
Inputs may be any that keep to these rules, and one draw needn't show every extreme that they name: `tile_pairs`: column 0 is a speaker block, column 1 a microphone block. The rows of one device (aligned blocks of 26 rows) all lie in that device's bin, and their speaker blocks s satisfy s // 2 = (device index) % 16; no pair repeats on a device. Counting microphone blocks m by the device m * 16 // 128, at most 4 rows of one device fall to any one device, and in every part one device gets exactly 4 from every device.
All inputs are finite; a program needn't handle non-finite values.
Results may differ from a plain program's by a relative error of at most 0.0032.
Values may be sent and summed in bfloat16 or wider, within the bound.
No kernel may reach another device: no remote copies, remote signals or barrier semaphores. Data moves between devices by JAX's collectives and lax.ppermute only.
A program may use at most 128 MiB of HBM per device.

v0:
```python
import jax
import jax.numpy as jnp
from jax import lax
from jax.sharding import PartitionSpec as P

SBLK = 32
MBLK = 128
SPEAKERS = 4096
reg_weight = 0.25


def complex_forward(plant, field_rows):
    halfway = field_rows.shape[-1] // 2
    product = jnp.einsum("tcij,tjk->tcik", plant, field_rows, preferred_element_type=jnp.float32)
    real_part = product[:, 0, :, :halfway] - product[:, 1, :, halfway:]
    imag_part = product[:, 0, :, halfway:] + product[:, 1, :, :halfway]
    return jnp.concatenate([real_part, imag_part], axis=-1)


def complex_adjoint(plant, field_rows):
    halfway = field_rows.shape[-1] // 2
    product = jnp.einsum("tcij,tik->tcjk", plant, field_rows, preferred_element_type=jnp.float32)
    real_part = product[:, 0, :, :halfway] + product[:, 1, :, halfway:]
    imag_part = product[:, 0, :, halfway:] - product[:, 1, :, :halfway]
    return jnp.concatenate([real_part, imag_part], axis=-1)


def per_device(direction, plant, tile_pairs, mic_weight):
    devices = lax.axis_size("spk")
    device_id = lax.axis_index("spk")
    unit_count = direction.shape[0]
    tile_count = plant.shape[0]
    block_size = direction.shape[1]
    field_width = direction.shape[2]
    groups_per_bin = SBLK // unit_count
    bin_count = devices // groups_per_bin
    peer_blocks = MBLK // devices
    mic_units = bin_count * peer_blocks
    my_bin = device_id // groups_per_bin
    local_unit = tile_pairs[:, 0] % unit_count
    mic_block = tile_pairs[:, 1]
    direction_rows = direction.astype(jnp.bfloat16)[local_unit]
    partial_field = complex_forward(plant, direction_rows)
    local_power = jnp.sum(jnp.square(plant.astype(jnp.float32)))
    power_terms = jnp.where(jnp.arange(bin_count) == my_bin, local_power, 0.0)
    bin_power = lax.psum(power_terms, "spk")
    weights_flat = mic_weight.reshape(mic_units, block_size)
    capacity = max(3, (2 * tile_count + devices - 1) // devices)
    target_peer = mic_block // peer_blocks
    peer_onehot = (target_peer[:, None] == jnp.arange(devices)[None, :]).astype(jnp.int32)
    running = jnp.cumsum(peer_onehot, axis=0)
    slot_rank = jnp.take_along_axis(running, target_peer[:, None], axis=1)[:, 0] - 1
    position = target_peer * capacity + slot_rank
    target_label = my_bin * peer_blocks + mic_block - target_peer * peer_blocks
    outgoing = (
        jnp.zeros((devices * capacity, block_size, field_width), jnp.float32)
        .at[position]
        .set(partial_field)
    )
    labels = jnp.full((devices * capacity,), mic_units, jnp.int32).at[position].set(target_label)
    labels_in = lax.all_to_all(
        labels.reshape(devices, capacity), "spk", split_axis=0, concat_axis=0, tiled=True
    )
    arrived = lax.all_to_all(
        outgoing.reshape(devices, capacity, block_size, field_width),
        "spk",
        split_axis=0,
        concat_axis=0,
        tiled=True,
    )
    flat_labels = labels_in.reshape(devices * capacity)
    pressure = jax.ops.segment_sum(
        arrived.reshape(devices * capacity, block_size, field_width),
        flat_labels,
        num_segments=mic_units + 1,
    )[:mic_units]
    weighted = (weights_flat[:, :, None] * pressure).astype(jnp.bfloat16)
    clipped = jnp.minimum(flat_labels, mic_units - 1)
    reply = weighted[clipped].reshape(devices, capacity, block_size, field_width)
    returned = lax.all_to_all(reply, "spk", split_axis=0, concat_axis=0, tiled=True)
    tile_weighted = returned.reshape(devices * capacity, block_size, field_width)[position]
    back_field = complex_adjoint(plant, tile_weighted)
    unit_onehot = (local_unit[:, None] == jnp.arange(unit_count)[None, :]).astype(jnp.float32)
    gram = jnp.einsum("tu,tjk->ujk", unit_onehot, back_field, precision=lax.Precision.HIGHEST)
    my_power = bin_power[my_bin]
    return gram + reg_weight * my_power / SPEAKERS * direction


def solution(mesh):
    placed = (
        P(("band", "spk"), None, None),
        P(("band", "spk"), None, None, None),
        P(("band", "spk"), None),
        P("band", "spk", None),
    )
    return jax.shard_map(
        per_device,
        mesh=mesh,
        in_specs=placed,
        out_specs=P(("band", "spk"), None, None),
        check_vma=False,
    )
```

profile of v0, /device:TPU:16, one launch (start us, length us, event | category | flops | bytes accessed | tf_op | source)
XLA Modules:
  0.0 212.3 jit_solution(8495858670104442344)
XLA Ops:
  0.0 0.0 copy-start
  0.0 0.8 fusion.16
  0.9 0.7 fusion.18
  1.5 0.1 fusion.9
  1.7 0.8 gather_fusion.3
  2.5 0.7 scatter_custom_fusion
  3.2 0.7 all_to_all.12
  3.9 6.2 %all-to-all-start = ((s32[16,1,4]{2,1,0:T(1,128)}), s32[16,1,4]{2,1,0:T(1,128)S(1)}, u32[]{:S(2)}, u32[]{:S(2)}) async-start(s32[16,1,4]{2,1,0:T(1,128)} %bitcast.10), calls=%async_computation | async-start | bytes 16384 | tf_op jit(solution)/shard_map/all_to_all | solution.py:61
  10.0 0.9 convert_element_type.14
  11.0 0.7 gather_fusion
  11.7 0.0 copy-done
  11.7 0.7 convolution_bitcast_fusion.1
  12.4 0.1 fusion.3
  12.5 0.1 fusion.5
  12.6 0.2 pad_maximum_fusion
  12.8 1.7 copy.38
  14.5 0.0 copy-start.1
  14.5 2.4 %broadcast_in_dim.9 = f32[64,128,128]{2,1,0:T(8,128)} broadcast(f32[]{:T(128)} %constant.79.clone.1), dimensions={} | broadcast | bytes 4194308 | tf_op jit(solution)/shard_map/broadcast_in_dim | solution.py:56
  16.9 0.0 copy-done.1
  16.9 5.4 %scatter_fusion = f32[64,128,128]{2,1,0:T(8,128)} fusion(f32[64,128,128]{2,1,0:T(8,128)} %broadcast_in_dim.9, s32[26]{0:T(128)S(1)} %fusion.15, f32[26,128,128]{2,1,0:T(8,128)S(1)} %copy-done.1), kind=kCustom, calls=%fused_computation.5 | custom fusion | bytes 5111912 | tf_op jit(solution)/shard_map/scatter | solution.py:58
  22.3 0.0 all-to-all-done
  22.3 6.0 %all-to-all-start.1 = ((f32[16,4,128,128]{3,2,1,0:T(8,128)}), f32[16,4,128,128]{3,2,1,0:T(8,128)}, u32[]{:S(2)}, u32[]{:S(2)}) async-start(f32[16,4,128,128]{3,2,1,0:T(8,128)} %bitcast.87), calls=%async_computation.1 | async-start | bytes 8388608 | tf_op jit(solution)/shard_map/all_to_all | solution.py:64
  28.3 0.5 broadcast.181
  28.9 0.7 minimum_reduce_fusion
  29.6 0.1 reshape.124
  29.6 0.1 reshape.132
  29.8 91.2 %all-to-all-done.1 = f32[16,4,128,128]{3,2,1,0:T(8,128)} async-done(((f32[16,4,128,128]{3,2,1,0:T(8,128)}), f32[16,4,128,128]{3,2,1,0:T(8,128)}, u32[]{:S(2)}, u32[]{:S(2)}) %all-to-all-start.1) | async-done | bytes 4194336 | tf_op jit(solution)/shard_map/all_to_all | solution.py:64
  121.1 0.0 copy-start.3
  121.1 8.8 %scatter_fusion.1 = f32[9,128,128]{2,1,0:T(8,128)S(1)} fusion(f32[9,128,128]{2,1,0:T(8,128)S(1)} %broadcast_in_dim.8, s32[64]{0:T(128)S(1)} %reshape.124, f32[64,128,128]{2,1,0:T(8,128)} %bitcast.17), kind=kCustom, calls=%fused_computation.6 | custom fusion | flops 1048576 | bytes 12583168 | tf_op jit(solution)/shard_map/scatter-add | solution.py:72
  129.9 0.0 copy-done.3
  129.9 0.2 fusion.8
  130.1 2.1 gather_fusion.1
  132.2 4.6 %all-to-all-start.2 = ((bf16[16,4,128,128]{3,2,1,0:T(8,128)(2,1)}), bf16[16,4,128,128]{3,2,1,0:T(8,128)(2,1)}, u32[]{:S(2)}, u32[]{:S(2)}) async-start(bf16[16,4,128,128]{3,2,1,0:T(8,128)(2,1)} %bitcast.88), calls=%async_computation.2 | async-start | bytes 4194304 | tf_op jit(solution)/shard_map/all_to_all | solution.py:80
  136.8 1.5 multiply_reduce_fusion
  138.9 64.1 %psum.7 = f32[1]{0:T(128)} all-reduce(f32[1]{0:T(128)} %bitcast.25), channel_id=1, replica_groups=mesh['band'=2,'spk'=16] {'spk'}, use_global_device_ids=true, to_apply=%region_5.6 | all-reduce | flops 1 | bytes 8 | tf_op jit(solution)/shard_map/psum | solution.py:46
  203.7 0.0 all-to-all-done.2
  203.7 2.3 %gather_fusion.2 = bf16[26,128,128]{2,1,0:T(8,128)(2,1)S(1)} fusion(bf16[64,128,128]{2,1,0:T(8,128)(2,1)} %bitcast.20, s32[1024]{0:T(1024)S(1)} %pad_clamp_fusion), kind=kCustom, calls=%fused_computation.2 | custom fusion | bytes 1704040 | tf_op jit(solution)/shard_map/gather | solution.py:81
  206.0 0.7 convolution_bitcast_fusion
  206.7 0.1 fusion
  206.8 0.1 fusion.2
  206.9 0.1 pad_maximum_fusion.1
  207.0 0.0 copy-start.2
  207.1 2.2 %copy.42 = f32[26,128,128]{2,0,1:T(8,128)} copy(f32[26,128,128]{1,2,0:T(8,128)S(1)} %pad_maximum_fusion.1) | data formatting | bytes 3407872 | tf_op jit(solution)/shard_map/concatenate | solution.py:25
  209.3 2.4 %fusion.10 = f32[2,128,128]{2,0,1:T(2,128)S(1)} fusion(f32[26,128,128]{2,0,1:T(8,128)} %copy.42, s32[26]{0:T(128)S(1)} %bitcast.90), kind=kOutput, calls=%fused_computation.41 | convolution fusion | flops 10223668 | bytes 1835112 | tf_op jit(solution)/shard_map/tu,tjk->ujk/dot_general | solution.py:84
  211.6 0.0 copy-done.2
  211.6 0.7 copy_add_fusion
  (10 shorter events, 0.1 us)
Async XLA Ops:
  0.0 11.7 %copy-start = (bf16[26,2,128,128]{3,2,1,0:T(8,128)(2,1)S(1)}, bf16[26,2,128,128]{3,2,1,0:T(8,128)(2,1)}, u32[]{:S(2)}) copy-start(bf16[26,2,128,128]{3,2,1,0:T(8,128)(2,1)} %param.5) | copy-start | bytes 5111812
  3.9 18.5 %all-to-all-start = ((s32[16,1,4]{2,1,0:T(1,128)}), s32[16,1,4]{2,1,0:T(1,128)S(1)}, u32[]{:S(2)}, u32[]{:S(2)}) async-start(s32[16,1,4]{2,1,0:T(1,128)} %bitcast.10), calls=%async_computation | async-start | bytes 16384 | tf_op jit(solution)/shard_map/all_to_all | solution.py:61
  14.5 2.4 %copy-start.1 = (f32[26,128,128]{2,1,0:T(8,128)S(1)}, f32[26,128,128]{2,1,0:T(8,128)}, u32[]{:S(2)}) copy-start(f32[26,128,128]{2,1,0:T(8,128)} %copy.38) | copy-start | bytes 5111812
  22.3 98.7 %all-to-all-start.1 = ((f32[16,4,128,128]{3,2,1,0:T(8,128)}), f32[16,4,128,128]{3,2,1,0:T(8,128)}, u32[]{:S(2)}, u32[]{:S(2)}) async-start(f32[16,4,128,128]{3,2,1,0:T(8,128)} %bitcast.87), calls=%async_computation.1 | async-start | bytes 8388608 | tf_op jit(solution)/shard_map/all_to_all | solution.py:64
  121.1 8.8 %copy-start.3 = (f32[1,8,128]{2,1,0:T(8,128)S(1)}, f32[1,8,128]{2,1,0:T(8,128)}, u32[]{:S(2)}) copy-start(f32[1,8,128]{2,1,0:T(8,128)} %param.7) | copy-start | bytes 12292
  132.2 71.5 %all-to-all-start.2 = ((bf16[16,4,128,128]{3,2,1,0:T(8,128)(2,1)}), bf16[16,4,128,128]{3,2,1,0:T(8,128)(2,1)}, u32[]{:S(2)}, u32[]{:S(2)}) async-start(bf16[16,4,128,128]{3,2,1,0:T(8,128)(2,1)} %bitcast.88), calls=%async_computation.2 | async-start | bytes 4194304 | tf_op jit(solution)/shard_map/all_to_all | solution.py:80
  207.0 4.6 %copy-start.2 = (f32[2,128,128]{2,1,0:T(8,128)S(1)}, f32[2,128,128]{2,1,0:T(8,128)}, u32[]{:S(2)}) copy-start(f32[2,128,128]{2,1,0:T(8,128)} %param.4) | copy-start | bytes 393220
where the time goes:
time: 213 us; the launch traced here: 212 us
  waiting for transfers between devices  91.3 us (43%)
  blocking collectives  64.1 us (30%)
  local copies, waits for them, and re-layouts  19.7 us (9%)
  starting transfers between devices  16.8 us (8%)
  other arithmetic  15.2 us (7%)
  matrix products  3.66 us (2%)
    all_to_all x1, waiting for transfers between devices, per_device(): lax.all_to_all(outgoing.reshape(devices, capacity, block_size, field_widt...  91.2 us
    psum x1, blocking collectives, per_device(): bin_power = lax.psum(power_terms, 'spk')  64.1 us
    scatter-add x1, other arithmetic, per_device(): jax.ops.segment_sum(arrived.reshape(devices * capacity, block_size, field...  8.78 us
    all_to_all x1, starting transfers between devices, per_device(): lax.all_to_all(labels.reshape(devices, capacity), 'spk', split_axis=0, co...  6.18 us
    all_to_all x1, starting transfers between devices, per_device(): lax.all_to_all(outgoing.reshape(devices, capacity, block_size, field_widt...  6.01 us
    scatter x1, local copies, waits for them, and re-layouts, per_device(): outgoing = jnp.zeros((devices * capacity, block_size, field_width), jnp.f...  5.43 us
    all_to_all x1, starting transfers between devices, per_device(): lax.all_to_all(reply, 'spk', split_axis=0, concat_axis=0, tiled=True)  4.59 us
  transfers between devices with their start and end apart: 3, of which 1 were waited for; matrix products, arithmetic and copies ran while one was open for 7% of the time, Pallas kernels for 0%

commit v1 on v0

--- a/solution.py
+++ b/solution.py
@@ -7,6 +7,23 @@
 MBLK = 128
 SPEAKERS = 4096
 reg_weight = 0.25
+
+
+def wrap_routes_all(tile_in, d0, state):
+    state_next = tile_in.shape
+    return jnp.moveaxis(
+        tile_in.reshape(*state_next[:d0], state, state_next[d0] // state, *state_next[d0 + 1 :]),
+        d0,
+        0,
+    )
+
+
+def layers_all_do(payload, k_dim):
+    payload = jnp.moveaxis(payload, 0, k_dim)
+    tile_out = payload.shape
+    return payload.reshape(
+        *tile_out[:k_dim], tile_out[k_dim] * tile_out[k_dim + 1], *tile_out[k_dim + 2 :]
+    )
 
 
 def complex_forward(plant, field_rows):
@@ -77,7 +94,18 @@
     weighted = (weights_flat[:, :, None] * pressure).astype(jnp.bfloat16)
     clipped = jnp.minimum(flat_labels, mic_units - 1)
     reply = weighted[clipped].reshape(devices, capacity, block_size, field_width)
-    returned = lax.all_to_all(reply, "spk", split_axis=0, concat_axis=0, tiled=True)
+    k_now, met_up = (lax.axis_size("spk"), lax.axis_index("spk"))
+    block_next = wrap_routes_all(reply, 0, k_now)
+    heap = [block_next[met_up]]
+    for at in range(1, k_now):
+        piece_next = block_next[met_up ^ at]
+        heap.append(
+            lax.ppermute(
+                piece_next, axis_name="spk", perm=[(to_i, to_i ^ at) for to_i in range(k_now)]
+            )
+        )
+    block_next = jnp.stack(heap, 0)[met_up ^ jnp.arange(k_now)]
+    returned = layers_all_do(block_next, 0)
     tile_weighted = returned.reshape(devices * capacity, block_size, field_width)[position]
     back_field = complex_adjoint(plant, tile_weighted)
     unit_onehot = (local_unit[:, None] == jnp.arange(unit_count)[None, :]).astype(jnp.float32)

time: 213 us -> 240 us (1.13); the launches traced: 212 us -> 237 us
  blocking collectives: 64.1 us -> 24.6 us
  waiting for transfers between devices: 91.3 us -> 118 us
  starting transfers between devices: 16.8 us -> 36.8 us
  local copies, waits for them, and re-layouts: 19.7 us -> 37 us
    psum x1, blocking collectives: 64.1 us -> 24.6 us  [per_device(): bin_power = lax.psum(power_terms, 'spk')]
    ppermute x0 -> x15, waiting for transfers between devices: none -> 28 us  [per_device(): lax.ppermute(piece_next, axis_name='spk', perm=[(to_i, to_i ^ at) for to_...]
    ppermute x0 -> x15, starting transfers between devices: none -> 24.6 us  [per_device(): lax.ppermute(piece_next, axis_name='spk', perm=[(to_i, to_i ^ at) for to_...]
    unnamed x9 -> x23, local copies, waits for them, and re-layouts: 0.02 us -> 10.1 us
    all_to_all x1 -> x0, starting transfers between devices: 4.59 us -> none  [per_device(): lax.all_to_all(reply, 'spk', split_axis=0, concat_axis=0, tiled=True)]
    gather x0 -> x1, local copies, waits for them, and re-layouts: none -> 3.7 us  [per_device(): block_next = jnp.stack(heap, 0)[met_up ^ jnp.arange(k_now)]]
    squeeze x0 -> x1, local copies, waits for them, and re-layouts: none -> 2.71 us  [per_device(): piece_next = block_next[met_up ^ at]]
  transfers between devices with their start and end apart: 3 -> 17, of which waited for: 1 -> 9; matrix products, arithmetic and copies ran while one was open for 7% -> 11% of each run, Pallas kernels for 0% -> 0%
where the time goes in v1:
time: 240 us; the launch traced here: 237 us
  waiting for transfers between devices  118 us (49%)
  local copies, waits for them, and re-layouts  37 us (15%)
  starting transfers between devices  36.8 us (15%)
  blocking collectives  24.6 us (10%)
  other arithmetic  15.3 us (6%)
  matrix products  3.66 us (2%)
    all_to_all x1, waiting for transfers between devices, per_device(): lax.all_to_all(outgoing.reshape(devices, capacity, block_size, field_widt...  89.7 us
    ppermute x15, waiting for transfers between devices, per_device(): lax.ppermute(piece_next, axis_name='spk', perm=[(to_i, to_i ^ at) for to_...  28 us
    ppermute x15, starting transfers between devices, per_device(): lax.ppermute(piece_next, axis_name='spk', perm=[(to_i, to_i ^ at) for to_...  24.6 us
    psum x1, blocking collectives, per_device(): bin_power = lax.psum(power_terms, 'spk')  24.6 us
    unnamed x23, local copies, waits for them, and re-layouts  10.1 us
    scatter-add x1, other arithmetic, per_device(): jax.ops.segment_sum(arrived.reshape(devices * capacity, block_size, field...  8.78 us
    all_to_all x1, starting transfers between devices, per_device(): lax.all_to_all(labels.reshape(devices, capacity), 'spk', split_axis=0, co...  6.18 us
    all_to_all x1, starting transfers between devices, per_device(): lax.all_to_all(outgoing.reshape(devices, capacity, block_size, field_widt...  5.96 us
  transfers between devices with their start and end apart: 17, of which 9 were waited for; matrix products, arithmetic and copies ran while one was open for 11% of the time, Pallas kernels for 0%

profile of v1, /device:TPU:16, one launch (start us, length us, event | category | flops | bytes accessed | tf_op | source)
XLA Modules:
  0.0 236.5 jit_solution(10305390986525498439)
XLA Ops:
  0.0 0.8 fusion.16
  0.9 0.7 fusion.19
  1.7 0.8 gather_fusion.4
  3.2 0.7 all_to_all.9
  3.9 6.2 %all-to-all-start = ((s32[16,1,4]{2,1,0:T(1,128)}), s32[16,1,4]{2,1,0:T(1,128)S(1)}, u32[]{:S(2)}, u32[]{:S(2)}) async-start(s32[16,1,4]{2,1,0:T(1,128)} %bitcast.10), calls=%async_computation | async-start | bytes 16384 | tf_op jit(solution)/shard_map/all_to_all | solution.py:78
  10.0 0.9 convert_element_type.14
  11.0 0.7 gather_fusion
  12.8 1.7 copy.38
  14.5 2.5 %broadcast_in_dim.9 = f32[64,128,128]{2,1,0:T(8,128)} broadcast(f32[]{:T(128)} %constant.50.clone.1), dimensions={} | broadcast | bytes 4194308 | tf_op jit(solution)/shard_map/broadcast_in_dim | solution.py:73
  17.0 5.5 %scatter_fusion = f32[64,128,128]{2,1,0:T(8,128)} fusion(f32[64,128,128]{2,1,0:T(8,128)} %broadcast_in_dim.9, s32[26]{0:T(128)S(1)} %fusion.15, f32[26,128,128]{2,1,0:T(8,128)S(1)} %copy-done.1), kind=kCustom, calls=%fused_computation.6 | custom fusion | bytes 5111912 | tf_op jit(solution)/shard_map/scatter | solution.py:75
  22.4 6.0 %all-to-all-start.1 = ((f32[16,4,128,128]{3,2,1,0:T(8,128)}), f32[16,4,128,128]{3,2,1,0:T(8,128)}, u32[]{:S(2)}, u32[]{:S(2)}) async-start(f32[16,4,128,128]{3,2,1,0:T(8,128)} %bitcast.150), calls=%async_computation.1 | async-start | bytes 8388608 | tf_op jit(solution)/shard_map/all_to_all | solution.py:81
  28.4 1.5 multiply_reduce_fusion
  30.5 0.7 minimum_reduce_fusion
  31.4 89.7 %all-to-all-done.1 = f32[16,4,128,128]{3,2,1,0:T(8,128)} async-done(((f32[16,4,128,128]{3,2,1,0:T(8,128)}), f32[16,4,128,128]{3,2,1,0:T(8,128)}, u32[]{:S(2)}, u32[]{:S(2)}) %all-to-all-start.1) | async-done | bytes 4194336 | tf_op jit(solution)/shard_map/all_to_all | solution.py:81
  121.1 8.8 %scatter_fusion.1 = f32[9,128,128]{2,1,0:T(8,128)S(1)} fusion(f32[9,128,128]{2,1,0:T(8,128)S(1)} %broadcast_in_dim.8, s32[64]{0:T(128)S(1)} %reshape.142, f32[64,128,128]{2,1,0:T(8,128)} %bitcast.17), kind=kCustom, calls=%fused_computation.7 | custom fusion | flops 1048576 | bytes 12583168 | tf_op jit(solution)/shard_map/scatter-add | solution.py:89
  130.1 2.1 gather_fusion.1
  132.3 2.7 %dynamic-slice_bitcast_fusion = (bf16[1,4,128,128]{3,2,1,0:T(8,128)(2,1)S(1)}, bf16[1,4,128,128]{3,2,1,0:T(8,128)(2,1)S(1)}, bf16[1,4,128,128]{3,2,1,0:T(8,128)(...) fusion(bf16[16,1,4,128,128]{4,3,2,0,1:T(8,128)(2,1)} %bitcast.1, ...), kind=kLoop, calls=%fused_computation.45 | loop fusion | bytes 4194368 | tf_op jit(solution)/shard_map/squeeze | solution.py:101
  135.6 24.6 %psum.7 = f32[1]{0:T(128)} all-reduce(f32[1]{0:T(128)} %bitcast.57), channel_id=1, replica_groups=mesh['band'=2,'spk'=16] {'spk'}, use_global_device_ids=true, to_apply=%region_5.6 | all-reduce | flops 1 | bytes 8 | tf_op jit(solution)/shard_map/psum | solution.py:63
  161.0 7.1 %collective-permute-start.3 = (bf16[1,4,128,128]{3,2,1,0:T(8,128)(2,1)S(1)}, bf16[1,4,128,128]{3,2,1,0:T(8,128)(2,1)S(1)}, u32[]{:S(2)}, u32[]{:S(2)}) collective-permute-start(bf16[1,4,128,128]{3,2,1,0:T(8,128)(2,1)S(1)} %get-tuple-element.22), channel_id=1, source_target_pairs={{0,4},{1,5},{2,6},{3,7},{4,0},{5,1},{6,2},{7,3},{8,12},{9,13},{10,... | collective-permute-start | bytes 393224 | tf_op jit(solution)/shard_map/ppermute | solution.py:103
  168.2 1.3 collective-permute-start.5
  169.4 1.6 bitcast_dynamic-update-slice_fusion.14
  171.0 1.6 collective-permute-start.6
  173.2 4.0 %collective-permute-start.7 = (bf16[1,4,128,128]{3,2,1,0:T(8,128)(2,1)S(1)}, bf16[1,4,128,128]{3,2,1,0:T(8,128)(2,1)S(1)}, u32[]{:S(2)}, u32[]{:S(2)}) collective-permute-start(bf16[1,4,128,128]{3,2,1,0:T(8,128)(2,1)S(1)} %get-tuple-element.18), channel_id=1, source_target_pairs={{0,8},{1,9},{2,10},{3,11},{4,12},{5,13},{6,14},{7,15},{8,0},{9,1},... | collective-permute-start | bytes 393224 | tf_op jit(solution)/shard_map/ppermute | solution.py:103
  177.3 0.7 bitcast_dynamic-update-slice_fusion.12
  177.9 1.6 collective-permute-start.8
  179.5 0.7 bitcast_dynamic-update-slice_fusion.11
  180.2 2.2 collective-permute-start.9
  183.0 2.3 collective-permute-start.10
  185.3 0.7 bitcast_dynamic-update-slice_fusion.9
  186.2 0.7 bitcast_dynamic-update-slice_fusion.8
  186.9 7.4 %collective-permute-done.7 = bf16[1,4,128,128]{3,2,1,0:T(8,128)(2,1)S(1)} collective-permute-done((bf16[1,4,128,128]{3,2,1,0:T(8,128)(2,1)S(1)}, bf16[1,4,128,128]{3,2,1,0:T(8,128)(2,1)S(1)}, u32[]{:S(2)}, u32[]{:S(2)}) %collective-permute-start.7) | collective-permute-done | bytes 131104 | tf_op jit(solution)/shard_map/ppermute | solution.py:103
  195.0 2.2 collective-permute-done.8
  197.1 3.6 %collective-permute-start.13 = (bf16[1,4,128,128]{3,2,1,0:T(8,128)(2,1)S(1)}, bf16[1,4,128,128]{3,2,1,0:T(8,128)(2,1)S(1)}, u32[]{:S(2)}, u32[]{:S(2)}) collective-permute-start(bf16[1,4,128,128]{3,2,1,0:T(8,128)(2,1)S(1)} %get-tuple-element.12), channel_id=1, source_target_pairs={{0,14},{1,15},{2,12},{3,13},{4,10},{5,11},{6,8},{7,9},{8,6},{9,7},... | collective-permute-start | bytes 393224 | tf_op jit(solution)/shard_map/ppermute | solution.py:103
  201.4 1.2 collective-permute-done.9
  203.1 0.7 bitcast_dynamic-update-slice_fusion.5
  203.8 4.6 %collective-permute-done.10 = bf16[1,4,128,128]{3,2,1,0:T(8,128)(2,1)S(1)} collective-permute-done((bf16[1,4,128,128]{3,2,1,0:T(8,128)(2,1)S(1)}, bf16[1,4,128,128]{3,2,1,0:T(8,128)(2,1)S(1)}, u32[]{:S(2)}, u32[]{:S(2)}) %collective-permute-start.10) | collective-permute-done | bytes 131104 | tf_op jit(solution)/shard_map/ppermute | solution.py:103
  209.0 7.2 %collective-permute-done.11 = bf16[1,4,128,128]{3,2,1,0:T(8,128)(2,1)S(1)} collective-permute-done((bf16[1,4,128,128]{3,2,1,0:T(8,128)(2,1)S(1)}, bf16[1,4,128,128]{3,2,1,0:T(8,128)(2,1)S(1)}, u32[]{:S(2)}, u32[]{:S(2)}) %collective-permute-start.11) | collective-permute-done | bytes 131104 | tf_op jit(solution)/shard_map/ppermute | solution.py:103
  216.2 0.7 bitcast_dynamic-update-slice_fusion.3
  216.9 1.0 collective-permute-done.12
  218.5 3.8 %collective-permute-done.13 = bf16[1,4,128,128]{3,2,1,0:T(8,128)(2,1)S(1)} collective-permute-done((bf16[1,4,128,128]{3,2,1,0:T(8,128)(2,1)S(1)}, bf16[1,4,128,128]{3,2,1,0:T(8,128)(2,1)S(1)}, u32[]{:S(2)}, u32[]{:S(2)}) %collective-permute-start.13) | collective-permute-done | bytes 131104 | tf_op jit(solution)/shard_map/ppermute | solution.py:103
  222.4 0.7 bitcast_dynamic-update-slice_fusion.1
  223.5 0.7 bitcast_dynamic-update-slice_fusion
  224.2 3.7 %gather_fusion.2 = bf16[16,4,128,128]{3,2,1,0:T(8,128)(2,1)} fusion(bf16[16,4,128,128]{3,2,1,0:T(8,128)(2,1)} %bitcast.153, s32[1024]{0:T(1024)S(1)} %pad_clamp_fusion.1), kind=kCustom, calls=%fused_computation.2 | custom fusion | bytes 4194368 | tf_op jit(solution)/shard_map/gather | solution.py:107
  227.9 2.3 gather_fusion.3
  230.2 0.7 convolution_bitcast_fusion
  231.3 2.2 copy.42
  233.5 2.4 fusion.10
  235.9 0.7 copy_add_fusion
  (54 shorter events, 8.7 us)
Async XLA Ops:
  0.0 11.7 %copy-start = (bf16[26,2,128,128]{3,2,1,0:T(8,128)(2,1)S(1)}, bf16[26,2,128,128]{3,2,1,0:T(8,128)(2,1)}, u32[]{:S(2)}) copy-start(bf16[26,2,128,128]{3,2,1,0:T(8,128)(2,1)} %param.5) | copy-start | bytes 5111812
  3.9 18.6 %all-to-all-start = ((s32[16,1,4]{2,1,0:T(1,128)}), s32[16,1,4]{2,1,0:T(1,128)S(1)}, u32[]{:S(2)}, u32[]{:S(2)}) async-start(s32[16,1,4]{2,1,0:T(1,128)} %bitcast.10), calls=%async_computation | async-start | bytes 16384 | tf_op jit(solution)/shard_map/all_to_all | solution.py:78
  14.5 2.5 %copy-start.1 = (f32[26,128,128]{2,1,0:T(8,128)S(1)}, f32[26,128,128]{2,1,0:T(8,128)}, u32[]{:S(2)}) copy-start(f32[26,128,128]{2,1,0:T(8,128)} %copy.38) | copy-start | bytes 5111812
  22.4 98.6 %all-to-all-start.1 = ((f32[16,4,128,128]{3,2,1,0:T(8,128)}), f32[16,4,128,128]{3,2,1,0:T(8,128)}, u32[]{:S(2)}, u32[]{:S(2)}) async-start(f32[16,4,128,128]{3,2,1,0:T(8,128)} %bitcast.150), calls=%async_computation.1 | async-start | bytes 8388608 | tf_op jit(solution)/shard_map/all_to_all | solution.py:81
  121.1 8.8 %copy-start.3 = (f32[1,8,128]{2,1,0:T(8,128)S(1)}, f32[1,8,128]{2,1,0:T(8,128)}, u32[]{:S(2)}) copy-start(f32[1,8,128]{2,1,0:T(8,128)} %param.7) | copy-start | bytes 12292
  135.0 33.2 %collective-permute-start = (bf16[1,4,128,128]{3,2,1,0:T(8,128)(2,1)}, bf16[1,4,128,128]{3,2,1,0:T(8,128)(2,1)}, u32[]{:S(2)}, u32[]{:S(2)}) collective-permute-start(bf16[1,4,128,128]{3,2,1,0:T(8,128)(2,1)} %get-tuple-element.25), channel_id=1, source_target_pairs={{0,1},{1,0},{2,3},{3,2},{4,5},{5,4},{6,7},{7,6},{8,9},{9,8},{10,11... | collective-permute-start | bytes 393224 | tf_op jit(solution)/shard_map/ppermute | solution.py:103
  160.8 10.1 %collective-permute-start.1 = (bf16[1,4,128,128]{3,2,1,0:T(8,128)(2,1)S(1)}, bf16[1,4,128,128]{3,2,1,0:T(8,128)(2,1)S(1)}, u32[]{:S(2)}, u32[]{:S(2)}) collective-permute-start(bf16[1,4,128,128]{3,2,1,0:T(8,128)(2,1)S(1)} %get-tuple-element.24), channel_id=1, source_target_pairs={{0,2},{1,3},{2,0},{3,1},{4,6},{5,7},{6,4},{7,5},{8,10},{9,11},{10,... | collective-permute-start | bytes 393224 | tf_op jit(solution)/shard_map/ppermute | solution.py:103
  160.9 12.3 %collective-permute-start.2 = (bf16[1,4,128,128]{3,2,1,0:T(8,128)(2,1)S(1)}, bf16[1,4,128,128]{3,2,1,0:T(8,128)(2,1)S(1)}, u32[]{:S(2)}, u32[]{:S(2)}) collective-permute-start(bf16[1,4,128,128]{3,2,1,0:T(8,128)(2,1)S(1)} %get-tuple-element.23), channel_id=1, source_target_pairs={{0,3},{1,2},{2,1},{3,0},{4,7},{5,6},{6,5},{7,4},{8,11},{9,10},{10,... | collective-permute-start | bytes 393224 | tf_op jit(solution)/shard_map/ppermute | solution.py:103
  161.0 16.9 %collective-permute-start.3 = (bf16[1,4,128,128]{3,2,1,0:T(8,128)(2,1)S(1)}, bf16[1,4,128,128]{3,2,1,0:T(8,128)(2,1)S(1)}, u32[]{:S(2)}, u32[]{:S(2)}) collective-permute-start(bf16[1,4,128,128]{3,2,1,0:T(8,128)(2,1)S(1)} %get-tuple-element.22), channel_id=1, source_target_pairs={{0,4},{1,5},{2,6},{3,7},{4,0},{5,1},{6,2},{7,3},{8,12},{9,13},{10,... | collective-permute-start | bytes 393224 | tf_op jit(solution)/shard_map/ppermute | solution.py:103
  168.1 12.0 %collective-permute-start.4 = (bf16[1,4,128,128]{3,2,1,0:T(8,128)(2,1)S(1)}, bf16[1,4,128,128]{3,2,1,0:T(8,128)(2,1)S(1)}, u32[]{:S(2)}, u32[]{:S(2)}) collective-permute-start(bf16[1,4,128,128]{3,2,1,0:T(8,128)(2,1)S(1)} %get-tuple-element.21), channel_id=1, source_target_pairs={{0,5},{1,4},{2,7},{3,6},{4,1},{5,0},{6,3},{7,2},{8,13},{9,12},{10,... | collective-permute-start | bytes 393224 | tf_op jit(solution)/shard_map/ppermute | solution.py:103
  168.2 14.8 %collective-permute-start.5 = (bf16[1,4,128,128]{3,2,1,0:T(8,128)(2,1)S(1)}, bf16[1,4,128,128]{3,2,1,0:T(8,128)(2,1)S(1)}, u32[]{:S(2)}, u32[]{:S(2)}) collective-permute-start(bf16[1,4,128,128]{3,2,1,0:T(8,128)(2,1)S(1)} %get-tuple-element.20), channel_id=1, source_target_pairs={{0,6},{1,7},{2,4},{3,5},{4,2},{5,3},{6,0},{7,1},{8,14},{9,15},{10,... | collective-permute-start | bytes 393224 | tf_op jit(solution)/shard_map/ppermute | solution.py:103
  171.0 15.0 %collective-permute-start.6 = (bf16[1,4,128,128]{3,2,1,0:T(8,128)(2,1)S(1)}, bf16[1,4,128,128]{3,2,1,0:T(8,128)(2,1)S(1)}, u32[]{:S(2)}, u32[]{:S(2)}) collective-permute-start(bf16[1,4,128,128]{3,2,1,0:T(8,128)(2,1)S(1)} %get-tuple-element.19), channel_id=1, source_target_pairs={{0,7},{1,6},{2,5},{3,4},{4,3},{5,2},{6,1},{7,0},{8,15},{9,14},{10,... | collective-permute-start | bytes 393224 | tf_op jit(solution)/shard_map/ppermute | solution.py:103
  173.2 21.1 %collective-permute-start.7 = (bf16[1,4,128,128]{3,2,1,0:T(8,128)(2,1)S(1)}, bf16[1,4,128,128]{3,2,1,0:T(8,128)(2,1)S(1)}, u32[]{:S(2)}, u32[]{:S(2)}) collective-permute-start(bf16[1,4,128,128]{3,2,1,0:T(8,128)(2,1)S(1)} %get-tuple-element.18), channel_id=1, source_target_pairs={{0,8},{1,9},{2,10},{3,11},{4,12},{5,13},{6,14},{7,15},{8,0},{9,1},... | collective-permute-start | bytes 393224 | tf_op jit(solution)/shard_map/ppermute | solution.py:103
  177.9 19.2 %collective-permute-start.8 = (bf16[1,4,128,128]{3,2,1,0:T(8,128)(2,1)S(1)}, bf16[1,4,128,128]{3,2,1,0:T(8,128)(2,1)S(1)}, u32[]{:S(2)}, u32[]{:S(2)}) collective-permute-start(bf16[1,4,128,128]{3,2,1,0:T(8,128)(2,1)S(1)} %get-tuple-element.17), channel_id=1, source_target_pairs={{0,9},{1,8},{2,11},{3,10},{4,13},{5,12},{6,15},{7,14},{8,1},{9,0},... | collective-permute-start | bytes 393224 | tf_op jit(solution)/shard_map/ppermute | solution.py:103
  180.2 22.4 %collective-permute-start.9 = (bf16[1,4,128,128]{3,2,1,0:T(8,128)(2,1)S(1)}, bf16[1,4,128,128]{3,2,1,0:T(8,128)(2,1)S(1)}, u32[]{:S(2)}, u32[]{:S(2)}) collective-permute-start(bf16[1,4,128,128]{3,2,1,0:T(8,128)(2,1)S(1)} %get-tuple-element.16), channel_id=1, source_target_pairs={{0,10},{1,11},{2,8},{3,9},{4,14},{5,15},{6,12},{7,13},{8,2},{9,3},... | collective-permute-start | bytes 393224 | tf_op jit(solution)/shard_map/ppermute | solution.py:103
  183.0 25.4 %collective-permute-start.10 = (bf16[1,4,128,128]{3,2,1,0:T(8,128)(2,1)S(1)}, bf16[1,4,128,128]{3,2,1,0:T(8,128)(2,1)S(1)}, u32[]{:S(2)}, u32[]{:S(2)}) collective-permute-start(bf16[1,4,128,128]{3,2,1,0:T(8,128)(2,1)S(1)} %get-tuple-element.15), channel_id=1, source_target_pairs={{0,11},{1,10},{2,9},{3,8},{4,15},{5,14},{6,13},{7,12},{8,3},{9,2},... | collective-permute-start | bytes 393224 | tf_op jit(solution)/shard_map/ppermute | solution.py:103
  185.9 30.3 %collective-permute-start.11 = (bf16[1,4,128,128]{3,2,1,0:T(8,128)(2,1)S(1)}, bf16[1,4,128,128]{3,2,1,0:T(8,128)(2,1)S(1)}, u32[]{:S(2)}, u32[]{:S(2)}) collective-permute-start(bf16[1,4,128,128]{3,2,1,0:T(8,128)(2,1)S(1)} %get-tuple-element.14), channel_id=1, source_target_pairs={{0,12},{1,13},{2,14},{3,15},{4,8},{5,9},{6,10},{7,11},{8,4},{9,5},... | collective-permute-start | bytes 393224 | tf_op jit(solution)/shard_map/ppermute | solution.py:103
  194.3 23.6 %collective-permute-start.12 = (bf16[1,4,128,128]{3,2,1,0:T(8,128)(2,1)S(1)}, bf16[1,4,128,128]{3,2,1,0:T(8,128)(2,1)S(1)}, u32[]{:S(2)}, u32[]{:S(2)}) collective-permute-start(bf16[1,4,128,128]{3,2,1,0:T(8,128)(2,1)S(1)} %get-tuple-element.13), channel_id=1, source_target_pairs={{0,13},{1,12},{2,15},{3,14},{4,9},{5,8},{6,11},{7,10},{8,5},{9,4},... | collective-permute-start | bytes 393224 | tf_op jit(solution)/shard_map/ppermute | solution.py:103
  197.1 25.2 %collective-permute-start.13 = (bf16[1,4,128,128]{3,2,1,0:T(8,128)(2,1)S(1)}, bf16[1,4,128,128]{3,2,1,0:T(8,128)(2,1)S(1)}, u32[]{:S(2)}, u32[]{:S(2)}) collective-permute-start(bf16[1,4,128,128]{3,2,1,0:T(8,128)(2,1)S(1)} %get-tuple-element.12), channel_id=1, source_target_pairs={{0,14},{1,15},{2,12},{3,13},{4,10},{5,11},{6,8},{7,9},{8,6},{9,7},... | collective-permute-start | bytes 393224 | tf_op jit(solution)/shard_map/ppermute | solution.py:103
  202.6 20.9 %collective-permute-start.14 = (bf16[1,4,128,128]{3,2,1,0:T(8,128)(2,1)S(1)}, bf16[1,4,128,128]{3,2,1,0:T(8,128)(2,1)S(1)}, u32[]{:S(2)}, u32[]{:S(2)}) collective-permute-start(bf16[1,4,128,128]{3,2,1,0:T(8,128)(2,1)S(1)} %get-tuple-element.11), channel_id=1, source_target_pairs={{0,15},{1,14},{2,13},{3,12},{4,11},{5,10},{6,9},{7,8},{8,7},{9,6},... | collective-permute-start | bytes 393224 | tf_op jit(solution)/shard_map/ppermute | solution.py:103
  231.3 4.6 %copy-start.2 = (f32[2,128,128]{2,1,0:T(8,128)S(1)}, f32[2,128,128]{2,1,0:T(8,128)}, u32[]{:S(2)}) copy-start(f32[2,128,128]{2,1,0:T(8,128)} %param.4) | copy-start | bytes 393220
